TPU v7x, 32 devices: a whole 2x2x4 slice. The times are simulated.
32 devices in a mesh: dp: 8 (over y, x, core), tensor: 4 (over z).
Axes of the slice: x: 2, y: 2, z: 4, core: 2. Of those that a mesh axis runs over, the one named last changes fastest.
Arguments:
- inputs: bfloat16 [16384, 768], P(('dp', 'tensor')), may hold values from -6 to 6
- cotangent: bfloat16 [16384, 768], P(('dp', 'tensor')), may hold values from -6 to 6
- lengths: int32 [128], P('dp'), may hold values from 25 to 128
- block_kind: int32 [32], P('dp'), may hold values from 0 to 1
- w_qkv: bfloat16 [2, 3, 768, 768], P(None, None, None, 'tensor'), may hold values from -0.3125 to 0.3125
- qv_bias: bfloat16 [2, 2, 768], P(None, None, 'tensor'), may hold values from -3 to 3
- w_out: bfloat16 [2, 768, 768], P(None, 'tensor'), may hold values from -0.625 to 0.625
- resid_bias: bfloat16 [2, 2, 768], replicated, may hold values from -3 to 3
- norm_gain: bfloat16 [2, 2, 768], replicated, may hold values from 0.5 to 1.5
- norm_shift: bfloat16 [2, 2, 768], replicated, may hold values from -2 to 2
- w_up: bfloat16 [2, 768, 3072], P(None, None, 'tensor'), may hold values from -0.21875 to 0.21875
- up_bias: bfloat16 [2, 3072], P(None, 'tensor'), may hold values from -3 to 3
- w_down: bfloat16 [2, 3072, 768], P(None, 'tensor'), may hold values from -0.15625 to 0.15625
Outputs:
- layer_out: bfloat16 [16384, 768], P(('dp', 'tensor'))
- input_grad: float32 [16384, 768], P(('dp', 'tensor'))
- grad_w_qkv: float32 [2, 3, 768, 768], P(None, None, None, 'tensor')
- grad_qv_bias: float32 [2, 2, 768], P(None, None, 'tensor')
- grad_w_out: float32 [2, 768, 768], P(None, 'tensor')
- grad_resid_bias: float32 [2, 2, 768], replicated
- grad_norm_gain: float32 [2, 2, 768], replicated
- grad_norm_shift: float32 [2, 2, 768], replicated
- grad_w_up: float32 [2, 768, 3072], P(None, None, 'tensor')
- grad_up_bias: float32 [2, 3072], P(None, 'tensor')
- grad_w_down: float32 [2, 3072, 768], P(None, 'tensor')
Inputs may be any that keep to these rules, and one draw needn't show every extreme that they name: lengths[s] is the number of real tokens of chain s; positions from lengths[s] on are padding and are never attended to. `block_kind`: block b holds chains b * 4 to (b+1) * 4 - 1, all heavy (0) or all light (1).
All inputs are finite; a program needn't handle non-finite values.
Results may differ from a plain program's by a relative error of at most 0.019.
The roundings to bfloat16 on the way count: a program that leaves them out, or rounds other values in their place, can miss the bound.
Values may be sent and summed in bfloat16 or wider, within the bound.
No kernel may reach another device: no remote copies, remote signals or barrier semaphores. Data moves between devices by JAX's collectives and lax.ppermute only.
A program may use at most 128 MiB of HBM per device.

v0:
```python
import jax
import jax.numpy as jnp
from jax import lax
from jax.sharding import PartitionSpec as P

HEAD_DIM = 64
CHAIN = 128
BLOCK_SEQS = 4
EPSILON = 1e-05
SQRT_HALF = 0.7071067811865476
INV_ROOT_TWO_PI = 0.3989422804014327


def norm_forward(row_data, gain_rows, shift_rows):
    mean_row = jnp.mean(row_data, axis=-1, keepdims=True)
    centred = row_data - mean_row
    var_row = jnp.mean(centred * centred, axis=-1, keepdims=True)
    inv_std = lax.rsqrt(var_row + EPSILON)
    unit_rows = centred * inv_std
    return (unit_rows * gain_rows + shift_rows, unit_rows, inv_std)


def norm_backward(grad_rows, gain_rows, unit_rows, inv_std):
    scaled = grad_rows * gain_rows
    mean_first = jnp.mean(scaled, axis=-1, keepdims=True)
    mean_second = jnp.mean(scaled * unit_rows, axis=-1, keepdims=True)
    return inv_std * (scaled - mean_first - unit_rows * mean_second)


def type_sum(kind_hot, values):
    return jnp.einsum("rt,rd->td", kind_hot, values, precision=lax.Precision.HIGHEST)


def gelu_slope(values):
    return 0.5 * (1.0 + lax.erf(values * SQRT_HALF)) + values * INV_ROOT_TWO_PI * jnp.exp(
        -0.5 * values * values
    )


def split_heads(row_data, heads_here):
    return row_data.reshape(BLOCK_SEQS, CHAIN, heads_here, HEAD_DIM)


def ffn_apply(up_w, ubias_w, down_w, row_blocks, kinds):

    def step(carry, packed):
        row_data, block_type = packed
        pre_act = jnp.dot(row_data, up_w[block_type], preferred_element_type=jnp.float32) + ubias_w[
            block_type
        ].astype(jnp.float32)
        activ = jax.nn.gelu(pre_act, approximate=False).astype(jnp.bfloat16)
        return (
            carry,
            (
                pre_act,
                activ,
                jnp.dot(activ, down_w[block_type], preferred_element_type=jnp.float32),
            ),
        )

    return lax.scan(step, 0, (row_blocks, kinds))[1]


def ffn_grad(up_w, ubias_w, down_w, row_blocks, grad_blocks, pre_blocks, activ_blocks, kinds):

    def step(accums, packed):
        acc_up, acc_ubias, acc_down = accums
        row_data, grad_rows, pre_act, activ, block_type = packed
        acc_down = acc_down.at[block_type].add(
            jnp.einsum("rf,rd->fd", activ, grad_rows, preferred_element_type=jnp.float32)
        )
        d_activ = jnp.einsum(
            "rd,fd->rf", grad_rows, down_w[block_type], preferred_element_type=jnp.float32
        ).astype(jnp.bfloat16)
        d_pre = (d_activ.astype(jnp.float32) * gelu_slope(pre_act)).astype(jnp.bfloat16)
        acc_up = acc_up.at[block_type].add(
            jnp.einsum("rd,rf->df", row_data, d_pre, preferred_element_type=jnp.float32)
        )
        acc_ubias = acc_ubias.at[block_type].add(jnp.sum(d_pre.astype(jnp.float32), axis=0))
        partial_back = jnp.einsum(
            "rf,df->rd", d_pre, up_w[block_type], preferred_element_type=jnp.float32
        )
        return ((acc_up, acc_ubias, acc_down), partial_back)

    zeros_ffn = (
        jnp.zeros(up_w.shape, jnp.float32),
        jnp.zeros(ubias_w.shape, jnp.float32),
        jnp.zeros(down_w.shape, jnp.float32),
    )
    return lax.scan(step, zeros_ffn, (row_blocks, grad_blocks, pre_blocks, activ_blocks, kinds))


def local(
    inputs,
    cotangent,
    lengths,
    block_kind,
    w_qkv,
    qv_bias,
    w_out,
    resid_bias,
    norm_gain,
    norm_shift,
    w_up,
    up_bias,
    w_down,
):
    tok_dev = inputs.shape[0]
    group_rows = tok_dev * lax.axis_size("tensor")
    block_rows = BLOCK_SEQS * CHAIN
    n_blocks = group_rows // block_rows
    heads_here = w_qkv.shape[3] // HEAD_DIM
    score_scale = HEAD_DIM ** (-0.5)
    highest = lax.Precision.HIGHEST
    row_block = (lax.axis_index("tensor") * tok_dev + jnp.arange(tok_dev)) // block_rows
    block_hot = row_block[:, None] == jnp.arange(n_blocks)[None, :]
    row_kind = jnp.sum(jnp.where(block_hot, block_kind[None, :], 0), axis=1)
    kind_hot = (row_kind[:, None] == jnp.arange(2)[None, :]).astype(jnp.float32)

    def pick(kind_table):
        return jnp.dot(kind_hot, kind_table.astype(jnp.float32), precision=highest)

    key_valid = jnp.arange(CHAIN)[None, :] < lengths[:, None]
    valid_blocks = key_valid.reshape(n_blocks, BLOCK_SEQS, CHAIN)

    def scores_of(query_rows, key_rows, valid_keys):
        raw_scores = (
            jnp.einsum(
                "sqhd,skhd->shqk",
                split_heads(query_rows, heads_here),
                split_heads(key_rows, heads_here),
                preferred_element_type=jnp.float32,
            )
            * score_scale
        )
        return jnp.where(valid_keys[:, None, None, :], raw_scores, -1e30)

    gathered = lax.all_gather(inputs, "tensor", axis=0, tiled=True)
    input_blocks = gathered.reshape(n_blocks, block_rows, -1)

    def attend_forward(accums, packed):
        row_data, valid_keys, block_type = packed
        projected = jnp.einsum(
            "rd,jde->jre", row_data, w_qkv[block_type], preferred_element_type=jnp.float32
        )
        bias_pair = qv_bias[block_type].astype(jnp.float32)
        query_rows = (projected[0] + bias_pair[0]).astype(jnp.bfloat16)
        key_rows = projected[1].astype(jnp.bfloat16)
        value_rows = (projected[2] + bias_pair[1]).astype(jnp.bfloat16)
        scores = scores_of(query_rows, key_rows, valid_keys)
        row_max = jnp.max(scores, axis=-1, keepdims=True)
        log_total = row_max[..., 0] + jnp.log(jnp.sum(jnp.exp(scores - row_max), axis=-1))
        attn_probs = jnp.exp(scores - log_total[..., None]).astype(jnp.bfloat16)
        mixed = jnp.einsum(
            "shqk,skhd->sqhd",
            attn_probs,
            split_heads(value_rows, heads_here),
            preferred_element_type=jnp.float32,
        )
        mixed = mixed.reshape(block_rows, -1).astype(jnp.bfloat16)
        partial_out = jnp.dot(mixed, w_out[block_type], preferred_element_type=jnp.float32)
        return (
            accums,
            (jnp.stack([query_rows, key_rows, value_rows]), log_total, mixed, partial_out),
        )

    unused, (kept_proj, kept_total, kept_mixed, attn_parts) = lax.scan(
        attend_forward, 0, (input_blocks, valid_blocks, block_kind)
    )
    attn_rows = lax.psum_scatter(
        attn_parts.reshape(group_rows, -1), "tensor", scatter_dimension=0, tiled=True
    )
    hidden_one = inputs.astype(jnp.float32) + attn_rows + pick(resid_bias[:, 0])
    gain_one = pick(norm_gain[:, 0])
    normed, unit_one, inv_one = norm_forward(hidden_one, gain_one, pick(norm_shift[:, 0]))
    normed_low = normed.astype(jnp.bfloat16)
    gathered_norm = lax.all_gather(normed_low, "tensor", axis=0, tiled=True)
    norm_blocks = gathered_norm.reshape(n_blocks, block_rows, -1)
    kept_pre, kept_activ, ffn_parts = ffn_apply(w_up, up_bias, w_down, norm_blocks, block_kind)
    ffn_rows = lax.psum_scatter(
        ffn_parts.reshape(group_rows, -1), "tensor", scatter_dimension=0, tiled=True
    )
    hidden_two = normed + ffn_rows + pick(resid_bias[:, 1])
    gain_two = pick(norm_gain[:, 1])
    output_rows, unit_two, inv_two = norm_forward(hidden_two, gain_two, pick(norm_shift[:, 1]))
    layer_out = output_rows.astype(jnp.bfloat16)
    grad_out = cotangent.astype(jnp.float32)
    d_two = norm_backward(grad_out, gain_two, unit_two, inv_two)
    d_two_low = d_two.astype(jnp.bfloat16)
    gathered_two = lax.all_gather(d_two_low, "tensor", axis=0, tiled=True)
    two_blocks = gathered_two.reshape(n_blocks, block_rows, -1)
    (acc_up, acc_ubias, acc_down), ffn_back_parts = ffn_grad(
        w_up, up_bias, w_down, norm_blocks, two_blocks, kept_pre, kept_activ, block_kind
    )
    d_normed = (
        lax.psum_scatter(
            ffn_back_parts.reshape(group_rows, -1), "tensor", scatter_dimension=0, tiled=True
        )
        + d_two
    )
    up_total, ubias_total, down_total = (acc_up, acc_ubias, acc_down)
    d_one = norm_backward(d_normed, gain_one, unit_one, inv_one)
    gain_grads = jnp.stack(
        [type_sum(kind_hot, d_normed * unit_one), type_sum(kind_hot, grad_out * unit_two)], axis=1
    )
    shift_grads = jnp.stack([type_sum(kind_hot, d_normed), type_sum(kind_hot, grad_out)], axis=1)
    rbias_grads = jnp.stack([type_sum(kind_hot, d_one), type_sum(kind_hot, d_two)], axis=1)
    gathered_one = lax.all_gather(d_one.astype(jnp.bfloat16), "tensor", axis=0, tiled=True)
    one_blocks = gathered_one.reshape(n_blocks, block_rows, -1)

    def attend_backward(accums, packed):
        acc_qkv, acc_qv, acc_out = accums
        row_data, grad_rows, valid_keys, kept_rows, log_total, mixed, block_type = packed
        acc_out = acc_out.at[block_type].add(
            jnp.einsum("re,rd->ed", mixed, grad_rows, preferred_element_type=jnp.float32)
        )
        d_mixed = jnp.einsum(
            "rd,ed->re", grad_rows, w_out[block_type], preferred_element_type=jnp.float32
        ).astype(jnp.bfloat16)
        scores = scores_of(kept_rows[0], kept_rows[1], valid_keys)
        attn_probs = jnp.exp(scores - log_total[..., None])
        d_mixed_heads = split_heads(d_mixed, heads_here)
        d_value = jnp.einsum(
            "shqk,sqhd->skhd",
            attn_probs.astype(jnp.bfloat16),
            d_mixed_heads,
            preferred_element_type=jnp.float32,
        )
        d_value = d_value.reshape(block_rows, -1).astype(jnp.bfloat16)
        d_probs = jnp.einsum(
            "sqhd,skhd->shqk",
            d_mixed_heads,
            split_heads(kept_rows[2], heads_here),
            preferred_element_type=jnp.float32,
        )
        prob_dot = jnp.sum(attn_probs * d_probs, axis=-1, keepdims=True)
        d_scores = (attn_probs * (d_probs - prob_dot)).astype(jnp.bfloat16)
        d_query = (
            jnp.einsum(
                "shqk,skhd->sqhd",
                d_scores,
                split_heads(kept_rows[1], heads_here),
                preferred_element_type=jnp.float32,
            )
            * score_scale
        )
        d_key = (
            jnp.einsum(
                "shqk,sqhd->skhd",
                d_scores,
                split_heads(kept_rows[0], heads_here),
                preferred_element_type=jnp.float32,
            )
            * score_scale
        )
        d_query = d_query.reshape(block_rows, -1).astype(jnp.bfloat16)
        d_key = d_key.reshape(block_rows, -1).astype(jnp.bfloat16)
        d_proj = jnp.stack([d_query, d_key, d_value])
        acc_qkv = acc_qkv.at[block_type].add(
            jnp.einsum("rd,jre->jde", row_data, d_proj, preferred_element_type=jnp.float32)
        )
        bias_sums = jnp.stack(
            [
                jnp.sum(d_query.astype(jnp.float32), axis=0),
                jnp.sum(d_value.astype(jnp.float32), axis=0),
            ]
        )
        acc_qv = acc_qv.at[block_type].add(bias_sums)
        partial_back = jnp.einsum(
            "jre,jde->rd", d_proj, w_qkv[block_type], preferred_element_type=jnp.float32
        )
        return ((acc_qkv, acc_qv, acc_out), partial_back)

    zeros_attn = (
        jnp.zeros(w_qkv.shape, jnp.float32),
        jnp.zeros(qv_bias.shape, jnp.float32),
        jnp.zeros(w_out.shape, jnp.float32),
    )
    (acc_qkv, acc_qv, acc_out), qkv_back_parts = lax.scan(
        attend_backward,
        zeros_attn,
        (input_blocks, one_blocks, valid_blocks, kept_proj, kept_total, kept_mixed, block_kind),
    )
    input_grad = (
        lax.psum_scatter(
            qkv_back_parts.reshape(group_rows, -1).astype(jnp.bfloat16),
            "tensor",
            scatter_dimension=0,
            tiled=True,
        ).astype(jnp.float32)
        + d_one
    )
    qkv_total, qv_total, out_total, up_total, ubias_total, down_total = lax.psum(
        (acc_qkv, acc_qv, acc_out, up_total, ubias_total, down_total), "dp"
    )
    rbias_total, gain_total, shift_total = lax.psum(
        (rbias_grads, gain_grads, shift_grads), ("dp", "tensor")
    )
    return (
        layer_out,
        input_grad,
        qkv_total,
        qv_total,
        out_total,
        rbias_total,
        gain_total,
        shift_total,
        up_total,
        ubias_total,
        down_total,
    )


def solution(mesh):
    return jax.shard_map(
        local,
        mesh=mesh,
        in_specs=(
            P(("dp", "tensor"), None),
            P(("dp", "tensor"), None),
            P("dp"),
            P("dp"),
            P(None, None, None, "tensor"),
            P(None, None, "tensor"),
            P(None, "tensor", None),
            P(),
            P(),
            P(),
            P(None, None, "tensor"),
            P(None, "tensor"),
            P(None, "tensor", None),
        ),
        out_specs=(
            P(("dp", "tensor"), None),
            P(("dp", "tensor"), None),
            P(None, None, None, "tensor"),
            P(None, None, "tensor"),
            P(None, "tensor", None),
            P(),
            P(),
            P(),
            P(None, None, "tensor"),
            P(None, "tensor"),
            P(None, "tensor", None),
        ),
        check_vma=False,
    )
```

profile of v0, /device:TPU:0, one launch (start us, length us, event | category | flops | bytes accessed | tf_op | source)
XLA Modules:
  0.0 1168.2 jit_solution(15813986910202748736)
XLA Ops:
  8.8 67.0 %all-gather.5.cloned.1.call-done = bf16[2048,768]{1,0:T(8,128)(2,1)} async-done(((bf16[512,768]{1,0:T(8,128)(2,1)}), bf16[2048,768]{1,0:T(8,128)(2,1)}) %all-gather.5.cloned.1.call-update) | async-done | bytes 3145744 | tf_op jit(solution)/shard_map/all_gather | solution.py:138
  79.0 39.6 %while.68 = (s32[]{:T(128)}, bf16[4,3,512,192]{2,3,1,0:T(8,128)(2,1)}, f32[4,4,3,128]{3,2,1,0:T(4,128)S(1)}, bf16[4,512,192]{1,2,0:T(8,128)(2,1)S(1)}, f32[4,512...) while((s32[]{:T(128)}, ...), condition=%wide.region_3.4_spmd, body=%wide.region_0.3_spmd.sunk | while | flops 658340736 | bytes 15210975 | solution.py:167
  120.6 107.5 %reduce-scatter.5.cloned.1.call-done = f32[512,768]{1,0:T(8,128)} async-done(((f32[2048,768]{1,0:T(8,128)}), f32[512,768]{1,0:T(8,128)}) %reduce-scatter.5.cloned.1.call-update) | async-done | bytes 1572880 | tf_op jit(solution)/shard_map/reduce_scatter | solution.py:170
  232.6 64.0 %all-gather.7.cloned.1.call-done = bf16[2048,768]{1,0:T(8,128)(2,1)} async-done(((bf16[512,768]{1,0:T(8,128)(2,1)}), bf16[2048,768]{1,0:T(8,128)(2,1)}) %all-gather.7.cloned.1.call-update) | async-done | bytes 3145744 | tf_op jit(solution)/shard_map/all_gather | solution.py:177
  303.0 48.6 %while.69 = (s32[]{:T(128)}, f32[4,512,768]{2,1,0:T(8,128)}, bf16[4,512,768]{2,1,0:T(8,128)(2,1)}, f32[4,512,768]{2,1,0:T(8,128)}, bf16[4,512,768]{2,1,0:T(8,128...) while((s32[]{:T(128)}, f32[4,512,768]{2,1,0:T(8,128)}, ...), condition=%wide.region_9.10_spmd, body=%wide.region_8.9_spmd.sunk | while | flops 1233912576 | bytes 21243096 | solution.py:61
  351.7 109.5 %reduce-scatter.7.cloned.1.call-done = f32[512,768]{1,0:T(8,128)} async-done(((f32[2048,768]{1,0:T(8,128)}), f32[512,768]{1,0:T(8,128)}) %reduce-scatter.7.cloned.1.call-update) | async-done | bytes 1572880 | tf_op jit(solution)/shard_map/reduce_scatter | solution.py:180
  467.7 63.9 %all-gather.9.cloned.1.call-done = bf16[2048,768]{1,0:T(8,128)(2,1)} async-done(((bf16[512,768]{1,0:T(8,128)(2,1)}), bf16[2048,768]{1,0:T(8,128)(2,1)}) %all-gather.9.cloned.1.call-update) | async-done | bytes 3145744 | tf_op jit(solution)/shard_map/all_gather | solution.py:190
  539.7 79.0 %while.70 = (s32[]{:T(128)}, f32[2,768,768]{2,1,0:T(8,128)}, f32[2,768]{1,0:T(2,128)S(1)}, f32[2,768,768]{2,1,0:T(8,128)}, f32[4,512,768]{2,1,0:T(8,128)}, /*ind...) while((s32[]{:T(128)}, f32[2,768,768]{2,1,0:T(8,128)}, ...), condition=%wide.region_19.20_spmd, body=%wide.region_15.19_spmd.sunk | while | flops 2423784192 | bytes 36199780 | solution.py:90
  546.1 4.7 fusion.226
  552.1 5.3 fusion.227
  565.8 4.7 fusion.226
  571.8 5.3 fusion.227
  585.6 4.7 fusion.226
  591.7 5.3 fusion.227
  605.3 4.7 fusion.226
  611.4 5.3 fusion.227
  619.2 109.0 %reduce-scatter.9.cloned.1.call-done = f32[512,768]{1,0:T(8,128)} async-done(((f32[2048,768]{1,0:T(8,128)}), f32[512,768]{1,0:T(8,128)}) %reduce-scatter.9.cloned.1.call-update) | async-done | bytes 1572880 | tf_op jit(solution)/shard_map/reduce_scatter | solution.py:196
  735.0 62.2 %all-gather.11.cloned.1.call-done = bf16[2048,768]{1,0:T(8,128)(2,1)} async-done(((bf16[512,768]{1,0:T(8,128)(2,1)}), bf16[2048,768]{1,0:T(8,128)(2,1)}) %all-gather.11.cloned.1.call-update) | async-done | bytes 3145744 | tf_op jit(solution)/shard_map/all_gather | solution.py:208
  800.4 95.7 %while.71 = (s32[]{:T(128)}, f32[2,3,768,192]{2,3,1,0:T(8,128)}, f32[2,2,192]{2,1,0:T(2,128)S(1)}, f32[2,192,768]{2,1,0:T(8,128)}, bf16[4,512,768]{2,1,0:T(8,128...) while((s32[]{:T(128)}, f32[2,3,768,192]{2,3,1,0:T(8,128)}, ...), condition=%wide.region_29.30_spmd, body=%wide.region_23.29_spmd.sunk | while | flops 1337720064 | bytes 39173132 | solution.py:279
  837.6 4.2 fusion.244
  905.5 43.0 %all-reduce = (f32[2,2,768]{2,0,1:T(2,128)S(1)}, f32[2,2,768]{2,0,1:T(2,128)S(1)}, f32[2,2,768]{2,0,1:T(2,128)S(1)}) all-reduce(f32[2,2,768]{2,0,1:T(2,128)S(1)} %pad_maximum_fusion, f32[2,2,768]{2,0,1:T(2,128)S(1)} %pad_maximum_fusion.1, f32[2,2,768]{2,0,1:T(2,128)S(1)} %pad_maximum_fusion.2), channel_id=1, replica_groups=mesh['dp'=8,'tensor'=4] {'dp','tensor'}, use_global_device_ids=true, to_apply=%region_34.35 | all-reduce | flops 9216 | bytes 73728 | tf_op jit(solution)/shard_map/psum | solution.py:296
  950.3 24.0 %all-reduce.1 = (f32[2,2,192]{2,1,0:T(2,128)}, f32[2,768]{1,0:T(2,128)}) all-reduce(f32[2,2,192]{2,1,0:T(2,128)S(1)} %get-tuple-element.342, f32[2,768]{1,0:T(2,128)S(1)} %copy-done.25), channel_id=1, replica_groups=mesh['dp'=8,'tensor'=4] {'dp'}, use_global_device_ids=true, to_apply=%region_32.33 | all-reduce | flops 2304 | bytes 18432 | tf_op jit(solution)/shard_map/psum | solution.py:293
  976.7 173.9 %all-reduce.5.cloned.1.call-done = (f32[2,3,768,192]{2,3,1,0:T(8,128)}, f32[2,192,768]{2,1,0:T(8,128)}, f32[2,768,768]{2,1,0:T(8,128)}, f32[2,768,768]{2,1,0:T(8,128)}) async-done(((f32[2,3,768,192]{2,3,1,0:T(8,128)}, f32[2,192,768]{2,1,0:T(8,128)}, f32[2,768,768]{2,1,0:T(8,128)}, f32[2,768,768]{2,1,0:T(8,128)}), (f32[2,3,768,192]{2,3,1,0:T(8,128)}, f32[2,192,768]{2,1,0:T(8,128)}, f32[2,768,768]{2,1,0:T(8,128)}, ...) | async-done | bytes 14155792 | tf_op jit(solution)/shard_map/psum | solution.py:293
  1150.6 4.3 copy.275
  (551 shorter events, 249.0 us)
Async XLA Ops:
  7.2 68.6 %all-gather.5.cloned.1.call-start = ((), (), s32[]{:S(2)}) async-start(), calls=%async_computation.4 | async-start | bytes 3932160 | tf_op jit(solution)/shard_map/all_gather | solution.py:138
  7.9 220.2 %reduce-scatter.5.cloned.1.call-start = ((), (), s32[]{:S(2)}) async-start(), calls=%async_computation.5 | async-start | bytes 7864320 | tf_op jit(solution)/shard_map/reduce_scatter | solution.py:170
  119.5 177.2 %all-gather.7.cloned.1.call-start = ((), (), s32[]{:S(2)}) async-start(), calls=%async_computation.6 | async-start | bytes 3932160 | tf_op jit(solution)/shard_map/all_gather | solution.py:177
  120.6 109.9 %copy-start.17 = (f32[512,768]{1,0:T(8,128)}, f32[512,768]{1,0:T(8,128)S(1)}, u32[]{:S(2)}) copy-start(f32[512,768]{1,0:T(8,128)S(1)} %fusion.116) | copy-start | bytes 4718596
  230.2 501.0 %copy-start = (f32[512,768]{1,0:T(8,128)}, f32[512,768]{1,0:T(8,128)S(1)}, u32[]{:S(2)}) copy-start(f32[512,768]{1,0:T(8,128)S(1)} %get-tuple-element.566) | copy-start | bytes 4718596
  230.2 501.0 %copy-start.29 = (f32[512]{0:T(512)}, f32[512]{0:T(512)S(1)}, u32[]{:S(2)}) copy-start(f32[512]{0:T(512)S(1)} %broadcast_multiply_fusion.5) | copy-start | bytes 6148
  230.6 500.7 %copy-start.33 = (f32[512]{0:T(512)}, f32[512]{0:T(512)S(1)}, u32[]{:S(2)}) copy-start(f32[512]{0:T(512)S(1)} %add_rsqrt_fusion.1) | copy-start | bytes 6148
  232.5 228.7 %reduce-scatter.7.cloned.1.call-start = ((), (), s32[]{:S(2)}) async-start(), calls=%async_computation.7 | async-start | bytes 7864320 | tf_op jit(solution)/shard_map/reduce_scatter | solution.py:180
  351.6 179.9 %all-gather.9.cloned.1.call-start = ((), (), s32[]{:S(2)}) async-start(), calls=%async_computation.8 | async-start | bytes 3932160 | tf_op jit(solution)/shard_map/all_gather | solution.py:190
  467.5 260.8 %reduce-scatter.9.cloned.1.call-start = ((), (), s32[]{:S(2)}) async-start(), calls=%async_computation.9 | async-start | bytes 7864320 | tf_op jit(solution)/shard_map/reduce_scatter | solution.py:196
  545.3 5.5 copy-start.9
  565.0 5.5 copy-start.9
  584.8 5.5 copy-start.9
  604.5 5.5 copy-start.9
  619.2 177.9 %all-gather.11.cloned.1.call-start = ((), (), s32[]{:S(2)}) async-start(), calls=%async_computation.10 | async-start | bytes 3932160 | tf_op jit(solution)/shard_map/all_gather | solution.py:208
  733.1 241.2 %reduce-scatter.11.cloned.1.call-start = ((), (), s32[]{:S(2)}) async-start(), calls=%async_computation.11 | async-start | bytes 3932160 | tf_op jit(solution)/shard_map/reduce_scatter | solution.py:285
  800.4 5.8 copy-start.35
  824.3 5.8 copy-start.35
  848.2 5.8 copy-start.35
  872.1 5.5 copy-start.49
  872.1 5.8 copy-start.35
  896.0 254.5 %all-reduce.5.cloned.1.call-start = ((), (), s32[]{:S(2)}) async-start(), calls=%async_computation.12 | async-start | bytes 28311552 | tf_op jit(solution)/shard_map/psum | solution.py:293
  904.6 45.6 %copy-start.25 = (f32[2,768]{1,0:T(2,128)S(1)}, f32[2,768]{1,0:T(2,128)}, u32[]{:S(2)}) copy-start(f32[2,768]{1,0:T(2,128)} %copy-done.24) | copy-start | bytes 18436
  904.7 69.6 %copy-start.15 = (f32[512,768]{1,0:T(8,128)S(1)}, f32[512,768]{1,0:T(8,128)}, u32[]{:S(2)}) copy-start(f32[512,768]{1,0:T(8,128)} %get-tuple-element.534) | copy-start | bytes 4718596
  (93 other events, 261.3 us)
Sparse Core Ops, SparseCore 0:
  9.6 66.1 all-gather.4
  118.7 109.3 reduce-scatter.4
  232.6 63.9 all-gather.6
  351.7 109.4 reduce-scatter.6
  467.6 63.9 all-gather.8
  618.8 109.4 reduce-scatter.8
  733.2 63.9 all-gather.10
  896.2 59.9 reduce-scatter.10
  961.4 189.1 all-reduce.4
where the time goes:
time: 1170 us
  waiting for transfers between devices  758 us (65%)
  matrix products  172 us (15%)
  local copies, waits for them, and re-layouts  73.4 us (6%)
  blocking collectives  67 us (6%)
  other arithmetic  50 us (4%)
  loops' own time  32.5 us (3%)
  between operations  14.2 us (1%)
    psum x1, waiting for transfers between devices, local(): lax.psum((acc_qkv, acc_qv, acc_out, up_total, ubias_total, down_total), '...  174 us
    reduce_scatter x1, waiting for transfers between devices, local(): lax.psum_scatter(ffn_parts.reshape(group_rows, -1), 'tensor', scatter_dim...  110 us
    reduce_scatter x1, waiting for transfers between devices, local(): lax.psum_scatter(ffn_back_parts.reshape(group_rows, -1), 'tensor', scatte...  109 us
    reduce_scatter x1, waiting for transfers between devices, local(): lax.psum_scatter(attn_parts.reshape(group_rows, -1), 'tensor', scatter_di...  107 us
    all_gather x1, waiting for transfers between devices, local(): gathered = lax.all_gather(inputs, 'tensor', axis=0, tiled=True)  67 us
    all_gather x1, waiting for transfers between devices, local(): gathered_norm = lax.all_gather(normed_low, 'tensor', axis=0, tiled=True)  64 us
    all_gather x1, waiting for transfers between devices, local(): gathered_two = lax.all_gather(d_two_low, 'tensor', axis=0, tiled=True)  63.9 us
    all_gather x1, waiting for transfers between devices, local(): lax.all_gather(d_one.astype(jnp.bfloat16), 'tensor', axis=0, tiled=True)  62.2 us
  transfers between devices with their start and end apart: 9, of which 8 were waited for; matrix products, arithmetic and copies ran while one was open for 1% of the time, Pallas kernels for 0%

commit v1 on v0

--- a/solution.py
+++ b/solution.py
@@ -1,3 +1,4 @@
+import functools
 import jax
 import jax.numpy as jnp
 from jax import lax
@@ -9,6 +10,41 @@
 EPSILON = 1e-05
 SQRT_HALF = 0.7071067811865476
 INV_ROOT_TWO_PI = 0.3989422804014327
+
+
+def stages_all_expand(body, ndim_at):
+    body = jnp.moveaxis(body, 0, ndim_at)
+    work_now = body.shape
+    r1 = body.reshape(
+        *work_now[:ndim_at], work_now[ndim_at] * work_now[ndim_at + 1], *work_now[ndim_at + 2 :]
+    )
+    return r1
+
+
+def map_column_in(content, along_axis):
+    top, found_now = (lax.axis_size(along_axis), lax.axis_index(along_axis))
+    current_value, f_now = (content[None], 1)
+    while f_now < top:
+        everything = lax.ppermute(
+            current_value, along_axis, [(src_i, src_i ^ f_now) for src_i in range(top)]
+        )
+        spare = found_now & f_now == 0
+        current_value = jnp.concatenate(
+            [
+                jnp.where(spare, current_value, everything),
+                jnp.where(spare, everything, current_value),
+            ]
+        )
+        f_now *= 2
+    return current_value
+
+
+def _trace_waves(mine_x, frame, d_out):
+    w1 = stages_all_expand(map_column_in(mine_x, frame), d_out)
+    return w1
+
+
+guide_point = functools.partial(_trace_waves, frame="tensor", d_out=0)
 
 
 def norm_forward(row_data, gain_rows, shift_rows):
@@ -205,7 +241,7 @@
     )
     shift_grads = jnp.stack([type_sum(kind_hot, d_normed), type_sum(kind_hot, grad_out)], axis=1)
     rbias_grads = jnp.stack([type_sum(kind_hot, d_one), type_sum(kind_hot, d_two)], axis=1)
-    gathered_one = lax.all_gather(d_one.astype(jnp.bfloat16), "tensor", axis=0, tiled=True)
+    gathered_one = guide_point(d_one.astype(jnp.bfloat16))
     one_blocks = gathered_one.reshape(n_blocks, block_rows, -1)
 
     def attend_backward(accums, packed):

time: 1170 us -> 1210 us (1.034)
  waiting for transfers between devices: 758 us -> 781 us
    ppermute x0 -> x2, waiting for transfers between devices: none -> 83.7 us  [map_column_in(): lax.ppermute(current_value, along_axis, [(src_i, src_i ^ f_now) for src_i...]
    all_gather x1 -> x0, waiting for transfers between devices: 62.2 us -> none  [local(): lax.all_gather(d_one.astype(jnp.bfloat16), 'tensor', axis=0, tiled=True)]
  transfers between devices with their start and end apart: 9 -> 10, of which waited for: 8 -> 9; matrix products, arithmetic and copies ran while one was open for 1% -> 1% of each run, Pallas kernels for 0% -> 0%
where the time goes in v1:
time: 1210 us
  waiting for transfers between devices  781 us (65%)
  matrix products  171 us (14%)
  local copies, waits for them, and re-layouts  78.7 us (7%)
  blocking collectives  67.8 us (6%)
  other arithmetic  59.5 us (5%)
  loops' own time  31.9 us (3%)
  between operations  14.5 us (1%)
    psum x1, waiting for transfers between devices, local(): lax.psum((acc_qkv, acc_qv, acc_out, up_total, ubias_total, down_total), '...  174 us
    reduce_scatter x1, waiting for transfers between devices, local(): lax.psum_scatter(ffn_parts.reshape(group_rows, -1), 'tensor', scatter_dim...  110 us
    reduce_scatter x1, waiting for transfers between devices, local(): lax.psum_scatter(ffn_back_parts.reshape(group_rows, -1), 'tensor', scatte...  109 us
    reduce_scatter x1, waiting for transfers between devices, local(): lax.psum_scatter(attn_parts.reshape(group_rows, -1), 'tensor', scatter_di...  108 us
    ppermute x2, waiting for transfers between devices, map_column_in(): lax.ppermute(current_value, along_axis, [(src_i, src_i ^ f_now) for src_i...  83.7 us
    all_gather x1, waiting for transfers between devices, local(): gathered = lax.all_gather(inputs, 'tensor', axis=0, tiled=True)  67 us
    all_gather x1, waiting for transfers between devices, local(): gathered_norm = lax.all_gather(normed_low, 'tensor', axis=0, tiled=True)  64 us
    all_gather x1, waiting for transfers between devices, local(): gathered_two = lax.all_gather(d_two_low, 'tensor', axis=0, tiled=True)  63.9 us
  transfers between devices with their start and end apart: 10, of which 9 were waited for; matrix products, arithmetic and copies ran while one was open for 1% of the time, Pallas kernels for 0%

profile of v1, /device:TPU:0, one launch (start us, length us, event | category | flops | bytes accessed | tf_op | source)
XLA Modules:
  0.0 1208.9 jit_solution(10340863823736230984)
XLA Ops:
  8.8 67.0 %all-gather.4.cloned.1.call-done = bf16[2048,768]{1,0:T(8,128)(2,1)} async-done(((bf16[512,768]{1,0:T(8,128)(2,1)}), bf16[2048,768]{1,0:T(8,128)(2,1)}) %all-gather.4.cloned.1.call-update) | async-done | bytes 3145744 | tf_op jit(solution)/shard_map/all_gather | solution.py:174
  79.0 43.5 %while.68 = (s32[]{:T(128)}, bf16[4,3,512,192]{2,3,1,0:T(8,128)(2,1)}, f32[4,4,3,128]{3,2,1,0:T(4,128)}, bf16[4,512,192]{1,2,0:T(8,128)(2,1)}, f32[4,512,768]{2,...) while((s32[]{:T(128)}, ...), condition=%wide.region_3.4_spmd, body=%wide.region_0.3_spmd.sunk | while | flops 658340736 | bytes 15204931 | solution.py:203
  124.3 107.8 %reduce-scatter.5.cloned.1.call-done = f32[512,768]{1,0:T(8,128)} async-done(((f32[2048,768]{1,0:T(8,128)}), f32[512,768]{1,0:T(8,128)}) %reduce-scatter.5.cloned.1.call-update) | async-done | bytes 1572880 | tf_op jit(solution)/shard_map/reduce_scatter | solution.py:206
  236.5 64.0 %all-gather.6.cloned.1.call-done = bf16[2048,768]{1,0:T(8,128)(2,1)} async-done(((bf16[512,768]{1,0:T(8,128)(2,1)}), bf16[2048,768]{1,0:T(8,128)(2,1)}) %all-gather.6.cloned.1.call-update) | async-done | bytes 3145744 | tf_op jit(solution)/shard_map/all_gather | solution.py:213
  306.9 48.7 %while.69 = (s32[]{:T(128)}, f32[4,512,768]{2,1,0:T(8,128)}, bf16[4,512,768]{2,1,0:T(8,128)(2,1)}, f32[4,512,768]{2,1,0:T(8,128)}, bf16[4,512,768]{2,1,0:T(8,128...) while((s32[]{:T(128)}, f32[4,512,768]{2,1,0:T(8,128)}, ...), condition=%wide.region_9.10_spmd, body=%wide.region_8.9_spmd.sunk | while | flops 1233912576 | bytes 21243096 | solution.py:97
  355.7 109.5 %reduce-scatter.7.cloned.1.call-done = f32[512,768]{1,0:T(8,128)} async-done(((f32[2048,768]{1,0:T(8,128)}), f32[512,768]{1,0:T(8,128)}) %reduce-scatter.7.cloned.1.call-update) | async-done | bytes 1572880 | tf_op jit(solution)/shard_map/reduce_scatter | solution.py:216
  471.7 63.9 %all-gather.8.cloned.1.call-done = bf16[2048,768]{1,0:T(8,128)(2,1)} async-done(((bf16[512,768]{1,0:T(8,128)(2,1)}), bf16[2048,768]{1,0:T(8,128)(2,1)}) %all-gather.8.cloned.1.call-update) | async-done | bytes 3145744 | tf_op jit(solution)/shard_map/all_gather | solution.py:226
  543.7 80.4 %while.70 = (s32[]{:T(128)}, f32[2,768,768]{2,1,0:T(8,128)}, f32[2,768]{1,0:T(2,128)S(1)}, f32[2,768,768]{2,1,0:T(8,128)}, f32[4,512,768]{2,1,0:T(8,128)}, /*ind...) while((s32[]{:T(128)}, f32[2,768,768]{2,1,0:T(8,128)}, ...), condition=%wide.region_19.20_spmd, body=%wide.region_15.19_spmd.sunk | while | flops 2423784192 | bytes 36199780 | solution.py:126
  550.2 4.8 fusion.225
  556.5 5.3 fusion.226
  570.2 4.8 fusion.225
  576.6 5.3 fusion.226
  590.4 4.8 fusion.225
  596.7 5.3 fusion.226
  610.5 4.8 fusion.225
  616.8 5.3 fusion.226
  624.7 109.0 %reduce-scatter.9.cloned.1.call-done = f32[512,768]{1,0:T(8,128)} async-done(((f32[2048,768]{1,0:T(8,128)}), f32[512,768]{1,0:T(8,128)}) %reduce-scatter.9.cloned.1.call-update) | async-done | bytes 1572880 | tf_op jit(solution)/shard_map/reduce_scatter | solution.py:232
  740.0 18.1 %collective-permute-done = bf16[1,512,768]{2,1,0:T(8,128)(2,1)} collective-permute-done((bf16[1,512,768]{2,1,0:T(8,128)(2,1)}, bf16[1,512,768]{2,1,0:T(8,128)(2,1)}, u32[]{:S(2)}, u32[]{:S(2)}) %collective-permute-start) | collective-permute-done | bytes 786464 | tf_op jit(solution)/shard_map/ppermute | solution.py:28
  765.5 65.7 %collective-permute-done.1 = bf16[2,512,768]{2,1,0:T(8,128)(2,1)} collective-permute-done((bf16[2,512,768]{2,1,0:T(8,128)(2,1)}, bf16[2,512,768]{2,1,0:T(8,128)(2,1)}, u32[]{:S(2)}, u32[]{:S(2)}) %collective-permute-start.1) | collective-permute-done | bytes 1572896 | tf_op jit(solution)/shard_map/ppermute | solution.py:28
  837.9 97.0 %while.71 = (s32[]{:T(128)}, f32[2,3,768,192]{2,3,1,0:T(8,128)}, f32[2,2,192]{2,1,0:T(2,128)S(1)}, f32[2,192,768]{2,1,0:T(8,128)}, bf16[4,512,768]{2,1,0:T(8,128...) while((s32[]{:T(128)}, f32[2,3,768,192]{2,3,1,0:T(8,128)}, ...), condition=%wide.region_29.30_spmd, body=%wide.region_23.29_spmd.sunk | while | flops 1337720064 | bytes 38976468 | solution.py:315
  944.6 43.8 %all-reduce = (f32[2,2,768]{2,0,1:T(2,128)S(1)}, f32[2,2,768]{2,0,1:T(2,128)S(1)}, f32[2,2,768]{2,0,1:T(2,128)S(1)}) all-reduce(f32[2,2,768]{2,0,1:T(2,128)S(1)} %pad_maximum_fusion.2, f32[2,2,768]{2,0,1:T(2,128)S(1)} %pad_maximum_fusion.3, f32[2,2,768]{2,0,1:T(2,128)S(1)} %pad_maximum_fusion.4), channel_id=1, replica_groups=mesh['dp'=8,'tensor'=4] {'dp','tensor'}, use_global_device_ids=true, to_apply=%region_34.35 | all-reduce | flops 9216 | bytes 73728 | tf_op jit(solution)/shard_map/psum | solution.py:332
  990.2 24.0 %all-reduce.1 = (f32[2,2,192]{2,1,0:T(2,128)}, f32[2,768]{1,0:T(2,128)}) all-reduce(f32[2,2,192]{2,1,0:T(2,128)S(1)} %get-tuple-element.342, f32[2,768]{1,0:T(2,128)S(1)} %copy-done.25), channel_id=1, replica_groups=mesh['dp'=8,'tensor'=4] {'dp'}, use_global_device_ids=true, to_apply=%region_32.33 | all-reduce | flops 2304 | bytes 18432 | tf_op jit(solution)/shard_map/psum | solution.py:329
  1016.6 174.4 %all-reduce.5.cloned.1.call-done = (f32[2,3,768,192]{2,3,1,0:T(8,128)}, f32[2,192,768]{2,1,0:T(8,128)}, f32[2,768,768]{2,1,0:T(8,128)}, f32[2,768,768]{2,1,0:T(8,128)}) async-done(((f32[2,3,768,192]{2,3,1,0:T(8,128)}, f32[2,192,768]{2,1,0:T(8,128)}, f32[2,768,768]{2,1,0:T(8,128)}, f32[2,768,768]{2,1,0:T(8,128)}), (f32[2,3,768,192]{2,3,1,0:T(8,128)}, f32[2,192,768]{2,1,0:T(8,128)}, f32[2,768,768]{2,1,0:T(8,128)}, ...) | async-done | bytes 14155792 | tf_op jit(solution)/shard_map/psum | solution.py:329
  1191.0 4.3 copy.275
  (548 shorter events, 270.9 us)
Async XLA Ops:
  7.2 68.6 %all-gather.4.cloned.1.call-start = ((), (), s32[]{:S(2)}) async-start(), calls=%async_computation.4 | async-start | bytes 3932160 | tf_op jit(solution)/shard_map/all_gather | solution.py:174
  7.9 224.2 %reduce-scatter.5.cloned.1.call-start = ((), (), s32[]{:S(2)}) async-start(), calls=%async_computation.5 | async-start | bytes 7864320 | tf_op jit(solution)/shard_map/reduce_scatter | solution.py:206
  123.1 177.5 %all-gather.6.cloned.1.call-start = ((), (), s32[]{:S(2)}) async-start(), calls=%async_computation.6 | async-start | bytes 3932160 | tf_op jit(solution)/shard_map/all_gather | solution.py:213
  124.3 110.3 %copy-start.17 = (f32[512,768]{1,0:T(8,128)}, f32[512,768]{1,0:T(8,128)S(1)}, u32[]{:S(2)}) copy-start(f32[512,768]{1,0:T(8,128)S(1)} %fusion.116) | copy-start | bytes 4718596
  234.2 502.4 %copy-start = (f32[512,768]{1,0:T(8,128)}, f32[512,768]{1,0:T(8,128)S(1)}, u32[]{:S(2)}) copy-start(f32[512,768]{1,0:T(8,128)S(1)} %get-tuple-element.570) | copy-start | bytes 4718596
  234.2 502.4 %copy-start.29 = (f32[512]{0:T(512)}, f32[512]{0:T(512)S(1)}, u32[]{:S(2)}) copy-start(f32[512]{0:T(512)S(1)} %broadcast_multiply_fusion.5) | copy-start | bytes 6148
  234.5 502.1 %copy-start.33 = (f32[512]{0:T(512)}, f32[512]{0:T(512)S(1)}, u32[]{:S(2)}) copy-start(f32[512]{0:T(512)S(1)} %add_rsqrt_fusion.1) | copy-start | bytes 6148
  236.5 228.7 %reduce-scatter.7.cloned.1.call-start = ((), (), s32[]{:S(2)}) async-start(), calls=%async_computation.7 | async-start | bytes 7864320 | tf_op jit(solution)/shard_map/reduce_scatter | solution.py:216
  355.6 179.9 %all-gather.8.cloned.1.call-start = ((), (), s32[]{:S(2)}) async-start(), calls=%async_computation.8 | async-start | bytes 3932160 | tf_op jit(solution)/shard_map/all_gather | solution.py:226
  471.5 262.2 %reduce-scatter.9.cloned.1.call-start = ((), (), s32[]{:S(2)}) async-start(), calls=%async_computation.9 | async-start | bytes 7864320 | tf_op jit(solution)/shard_map/reduce_scatter | solution.py:232
  549.3 5.6 copy-start.9
  569.4 5.6 copy-start.9
  589.6 5.6 copy-start.9
  609.6 5.6 copy-start.9
  624.7 389.5 %reduce-scatter.11.cloned.1.call-start = ((), (), s32[]{:S(2)}) async-start(), calls=%async_computation.10 | async-start | bytes 3932160 | tf_op jit(solution)/shard_map/reduce_scatter | solution.py:321
  738.5 19.5 %collective-permute-start = (bf16[1,512,768]{2,1,0:T(8,128)(2,1)}, bf16[1,512,768]{2,1,0:T(8,128)(2,1)}, u32[]{:S(2)}, u32[]{:S(2)}) collective-permute-start(bf16[1,512,768]{2,1,0:T(8,128)(2,1)} %get-tuple-element.533), channel_id=1, source_target_pairs={{0,1},{1,0},{2,3},{3,2},{4,5},{5,4},{6,7},{7,6},{8,9},{9,8},{10,11... | collective-permute-start | bytes 2359304 | tf_op jit(solution)/shard_map/ppermute | solution.py:28
  760.8 70.4 %collective-permute-start.1 = (bf16[2,512,768]{2,1,0:T(8,128)(2,1)}, bf16[2,512,768]{2,1,0:T(8,128)(2,1)}, u32[]{:S(2)}, u32[]{:S(2)}) collective-permute-start(bf16[2,512,768]{2,1,0:T(8,128)(2,1)} %pad_maximum_fusion.1), channel_id=1, source_target_pairs={{0,2},{1,3},{2,0},{3,1},{4,6},{5,7},{6,4},{7,5},{8,10},{9,11},{10,... | collective-permute-start | bytes 4718600 | tf_op jit(solution)/shard_map/ppermute | solution.py:28
  837.9 5.3 copy-start.48
  886.4 5.3 copy-start.48
  910.7 5.3 copy-start.48
  935.0 256.0 %all-reduce.5.cloned.1.call-start = ((), (), s32[]{:S(2)}) async-start(), calls=%async_computation.11 | async-start | bytes 28311552 | tf_op jit(solution)/shard_map/psum | solution.py:329
  943.8 46.4 %copy-start.25 = (f32[2,768]{1,0:T(2,128)S(1)}, f32[2,768]{1,0:T(2,128)}, u32[]{:S(2)}) copy-start(f32[2,768]{1,0:T(2,128)} %copy-done.24) | copy-start | bytes 18436
  943.8 70.4 %copy-start.15 = (f32[512,768]{1,0:T(8,128)S(1)}, f32[512,768]{1,0:T(8,128)}, u32[]{:S(2)}) copy-start(f32[512,768]{1,0:T(8,128)} %get-tuple-element.534) | copy-start | bytes 4718596
  1191.0 5.4 copy-start.22
  (90 other events, 253.9 us)
Sparse Core Ops, SparseCore 0:
  9.6 66.1 all-gather.3
  122.7 109.3 reduce-scatter.4
  236.6 63.9 all-gather.5
  355.7 109.4 reduce-scatter.6
  471.6 63.9 all-gather.7
  624.2 109.4 reduce-scatter.8
  935.1 61.4 reduce-scatter.10
  1001.8 189.1 all-reduce.4
